TPU v7x, 32 devices: a whole 2x2x4 slice. The times are simulated.
32 devices in a mesh: group: 2 (over x), strip: 16 (over z, y, core).
Axes of the slice: x: 2, y: 2, z: 4, core: 2. Of those that a mesh axis runs over, the one named last changes fastest.
Arguments:
- strip_fields: float32 [3, 64, 128, 128], P(None, ('group', 'strip')), may hold values from -18 to 18
- strip_riser: int32 [64, 1], P('group'), may hold values from 0 to 3; in each aligned block of 2 rows (0 to 1, 2 to 3, ...) at most 2 rows name the same one
- strip_node: int32 [64], P('group'), may hold values from 0 to 1023
- riser_owner: int32 [2, 4], P('group'), may hold values from 0 to 15, as said below
- pivot_inv: float32 [32, 8, 128, 128], P(('group', 'strip')), may hold values from -0.2 to 1
- lower_block: float32 [32, 7, 128, 128], P(('group', 'strip')), may hold values from -0.109375 to 0.109375
- upper_block: float32 [32, 7, 128, 128], P(('group', 'strip')), may hold values from -0.109375 to 0.109375
Outputs:
- vorticity: float32 [64, 128, 128], P(('group', 'strip'))
- displacement: float32 [32, 16, 1024], P(('group', 'strip'))
Inputs may be any that keep to these rules, and one draw needn't show every extreme that they name: `strip_riser`: in each aligned block of 2 strips (the strips of one device) no riser is named more than 2 times, and some block names one riser exactly 2 times. `riser_owner`: the 4 owners in a row are distinct devices.
All inputs are finite; a program needn't handle non-finite values.
Results may differ from a plain program's by a relative error of at most 0.0003.
Values sent between devices are 32-bit elements; how exact they have to be, the bound alone decides.
No kernel may reach another device: no remote copies, remote signals or barrier semaphores. Data moves between devices by JAX's collectives and lax.ppermute only.
A program may use at most 64 MiB of HBM per device.

v0:
```python
import jax
import jax.numpy as jnp
from jax import lax
from jax.sharding import PartitionSpec as P

NSUB = 8
COUPLED = 2
TIME_STEP = 0.25
VISCOSITY = 0.05
COUPLING = 0.5
EXACT_DOT = lax.Precision.HIGHEST


def make_kernels(grid_cells):
    centre = jnp.arange(grid_cells, dtype=jnp.float32) - grid_cells / 2.0 + 0.5
    near_x = (centre / (grid_cells / 16.0))[None, :]
    near_y = (centre / (grid_cells / 16.0))[:, None]
    bell_near = jnp.exp(-(near_x * near_x + near_y * near_y) / 2.0)
    source_x = -near_x * bell_near
    source_y = -near_y * bell_near
    wide_x = (centre / (grid_cells / 8.0))[None, :]
    wide_y = (centre / (grid_cells / 8.0))[:, None]
    bell_wide = jnp.exp(-(wide_x * wide_x + wide_y * wide_y) / 2.0)
    lift_kernel = -wide_x * bell_wide
    drag_kernel = wide_y * bell_wide
    lift_kernel = lift_kernel / jnp.sqrt(jnp.sum(lift_kernel * lift_kernel))
    drag_kernel = drag_kernel / jnp.sqrt(jnp.sum(drag_kernel * drag_kernel))
    return (source_x, source_y, lift_kernel, drag_kernel)


def strip_step(vorticity, flow_x, flow_y, motion, kernels, substeps):
    source_x, source_y, lift_kernel, drag_kernel = kernels
    halves = motion.reshape(motion.shape[0], 2, substeps)
    earlier = jnp.concatenate([jnp.zeros_like(halves[:, :, :1]), halves[:, :, :-1]], axis=2)
    velocity = halves - earlier
    lift_rows = []
    drag_rows = []
    for substep in range(substeps):
        right_cell = jnp.roll(vorticity, -1, axis=2)
        left_cell = jnp.roll(vorticity, 1, axis=2)
        upper_cell = jnp.roll(vorticity, -1, axis=1)
        lower_cell = jnp.roll(vorticity, 1, axis=1)
        laplacian = right_cell + left_cell + upper_cell + lower_cell - 4.0 * vorticity
        tendency = (
            VISCOSITY * laplacian
            - flow_x * (0.5 * (right_cell - left_cell))
            - flow_y * (0.5 * (upper_cell - lower_cell))
        )
        forcing = (
            velocity[:, 0, substep][:, None, None] * source_x
            - velocity[:, 1, substep][:, None, None] * source_y
        )
        vorticity = vorticity + TIME_STEP * tendency + COUPLING * forcing
        lift_rows.append(jnp.sum(vorticity * lift_kernel, axis=(1, 2)))
        drag_rows.append(jnp.sum(vorticity * drag_kernel, axis=(1, 2)))
    return (vorticity, jnp.stack(lift_rows + drag_rows, axis=1))


def apply_block(vectors, matrix):
    return lax.dot_general(vectors, matrix, (((1,), (1,)), ((), ())), precision=EXACT_DOT)


def first_contract(left_side, right_side):
    return lax.dot_general(left_side, right_side, (((0,), (0,)), ((), ())), precision=EXACT_DOT)


def beam_solve(beam_load, pivot_inv, lower_block, upper_block):
    block_count = pivot_inv.shape[0]
    block_size = pivot_inv.shape[1]
    blocks = beam_load.reshape(beam_load.shape[0], block_count, block_size)
    carried = [blocks[:, 0]]
    for block_index in range(1, block_count):
        pivoted = apply_block(carried[-1], pivot_inv[block_index - 1])
        carried.append(blocks[:, block_index] - apply_block(pivoted, lower_block[block_index - 1]))
    solved = [apply_block(carried[-1], pivot_inv[block_count - 1])]
    for block_index in range(block_count - 2, -1, -1):
        remainder = carried[block_index] - apply_block(solved[0], upper_block[block_index])
        solved.insert(0, apply_block(remainder, pivot_inv[block_index]))
    return jnp.concatenate(solved, axis=1)


def local(strip_fields, strip_riser, strip_node, riser_owner, pivot_inv, lower_block, upper_block):
    devices = lax.axis_size("strip")
    position = lax.axis_index("strip")
    per_device = strip_fields.shape[1]
    grid_cells = strip_fields.shape[2]
    node_count = pivot_inv.shape[1] * pivot_inv.shape[2]
    riser_count = riser_owner.shape[1]
    substeps = NSUB
    total_strips = per_device * devices * lax.axis_size("group")
    kernels = make_kernels(grid_cells)
    riser_match = (
        strip_riser[:, 0][:, None] == jnp.arange(riser_count, dtype=jnp.int32)[None, :]
    ).astype(jnp.int32)
    owner_index = jnp.sum(riser_match * riser_owner[0][None, :], axis=1)
    owned_here = owner_index == position
    node_hit = (
        owned_here[:, None]
        & (strip_node[:, None] == jnp.arange(node_count, dtype=jnp.int32)[None, :])
    ).astype(jnp.float32)
    local_owner = lax.dynamic_slice_in_dim(owner_index, position * per_device, per_device)
    local_node = lax.dynamic_slice_in_dim(strip_node, position * per_device, per_device)
    top_taper = 1.0 - jnp.arange(node_count, dtype=jnp.float32) / node_count
    vorticity = strip_fields[0]
    flow_x = strip_fields[1]
    flow_y = strip_fields[2]
    motion = jnp.zeros((per_device, 2 * substeps), jnp.float32)
    displacement = jnp.zeros((2 * substeps, node_count), jnp.float32)
    for coupled_step in range(COUPLED):
        vorticity, force_rows = strip_step(vorticity, flow_x, flow_y, motion, kernels, substeps)
        partial_drag = jnp.sum(force_rows[:, substeps:], axis=0)
        total_drag = lax.psum(partial_drag, ("group", "strip"))
        offset = total_drag / jnp.sqrt(jnp.float32(total_strips))
        beam_load = first_contract(
            lax.all_gather(force_rows, "strip", axis=0, tiled=True), node_hit
        )
        displacement = beam_solve(beam_load, pivot_inv[0], lower_block[0], upper_block[0])
        displacement = displacement.at[substeps:, :].add(offset[:, None] * top_taper[None, :])
        if coupled_step + 1 < COUPLED:
            every_owner = lax.all_gather(displacement[None], "strip", axis=0, tiled=True)
            chosen = jnp.take(every_owner, local_owner, axis=0)
            node_pick = jnp.broadcast_to(local_node[:, None, None], (per_device, 2 * substeps, 1))
            motion = jnp.take_along_axis(chosen, node_pick, axis=2)[:, :, 0]
    return (vorticity, displacement[None])


def solution(mesh):
    in_specs = (
        P(None, ("group", "strip"), None, None),
        P("group", None),
        P("group"),
        P("group", None),
        P(("group", "strip"), None, None, None),
        P(("group", "strip"), None, None, None),
        P(("group", "strip"), None, None, None),
    )
    out_specs = (P(("group", "strip"), None, None), P(("group", "strip"), None, None))
    return jax.shard_map(local, mesh=mesh, in_specs=in_specs, out_specs=out_specs, check_vma=False)
```

profile of v0, /device:TPU:0, one launch (start us, length us, event | category | flops | bytes accessed | tf_op | source)
XLA Modules:
  0.0 231.5 jit_solution(9136430588047142506)
XLA Ops:
  15.9 42.0 %psum.14 = f32[8]{0:T(128)S(1)} all-reduce(f32[8]{0:T(128)S(1)} %reduce_sum.352), channel_id=1, replica_groups=mesh['group'=2,'strip'=16] {'group','strip'}, use_global_device_ids=true, to_apply=%region_20.21 | all-reduce | flops 8 | bytes 64 | tf_op jit(solution)/shard_map/psum | solution.py:112
  58.8 21.0 %all-gather = f32[16,2,16]{2,1,0:T(2,128)S(1)} all-gather(f32[1,2,16]{2,1,0:T(2,128)S(1)} %bitcast.564), channel_id=1, replica_groups=mesh['group'=2,'strip'=16] {'strip'}, dimensions={0}, use_global_device_ids=true | all-gather | bytes 2176 | tf_op jit(solution)/shard_map/all_gather | solution.py:115
  82.5 1.1 convolution_subtract_fusion.27
  83.6 1.1 fusion.159
  84.7 1.1 convolution_subtract_fusion.26
  85.8 1.1 fusion.149
  86.9 1.1 convolution_subtract_fusion.25
  88.0 1.1 fusion.139
  89.0 1.1 convolution_subtract_fusion.24
  90.1 1.1 fusion.129
  91.2 1.1 convolution_subtract_fusion.23
  92.2 1.1 fusion.119
  93.3 1.1 convolution_subtract_fusion.22
  94.3 1.1 fusion.109
  95.4 1.1 convolution_subtract_fusion.21
  96.5 1.1 fusion.99
  102.2 33.8 %all-gather.4.cloned.1.call-done = f32[16,16,1024]{2,1,0:T(8,128)} async-done(((f32[1,16,1024]{2,1,0:T(8,128)}), f32[16,16,1024]{2,1,0:T(8,128)}) %all-gather.4.cloned.1.call-update) | async-done | bytes 1048592 | tf_op jit(solution)/shard_map/all_gather | solution.py:120
  136.0 1.8 gather_fusion
  142.2 1.1 multiply_reduce_fusion.7
  144.2 38.9 %psum.15 = f32[8]{0:T(128)S(1)} all-reduce(f32[8]{0:T(128)S(1)} %reduce_sum.369), channel_id=1, replica_groups=mesh['group'=2,'strip'=16] {'group','strip'}, use_global_device_ids=true, to_apply=%region_38.39 | all-reduce | flops 8 | bytes 64 | tf_op jit(solution)/shard_map/psum | solution.py:112
  183.9 20.6 %all-gather.1 = f32[16,2,16]{2,1,0:T(2,128)S(1)} all-gather(f32[1,2,16]{2,1,0:T(2,128)S(1)} %bitcast.565), channel_id=1, replica_groups=mesh['group'=2,'strip'=16] {'strip'}, dimensions={0}, use_global_device_ids=true | all-gather | bytes 2176 | tf_op jit(solution)/shard_map/all_gather | solution.py:115
  205.8 1.1 convolution_subtract_fusion.13
  206.9 1.1 fusion.155
  208.0 1.1 convolution_subtract_fusion.12
  210.1 1.1 convolution_subtract_fusion.11
  211.2 1.1 fusion.135
  212.2 1.1 convolution_subtract_fusion.10
  213.3 1.1 fusion.125
  214.3 1.1 convolution_subtract_fusion.9
  216.5 1.1 convolution_subtract_fusion.8
  218.6 1.1 convolution_subtract_fusion.7
  219.6 1.1 fusion.97
  (220 shorter events, 29.4 us)
Async XLA Ops:
  7.2 128.8 %all-gather.4.cloned.1.call-start = ((), (), s32[]{:S(2)}) async-start(), calls=%async_computation | async-start | bytes 1114112 | tf_op jit(solution)/shard_map/all_gather | solution.py:120
  8.3 1.0 copy-start
  79.8 0.7 copy-start.6
  79.8 0.7 copy-start.7
  80.5 0.7 copy-start.5
  84.7 12.9 %copy-start.2 = (f32[1,7,128,128]{3,2,1,0:T(8,128)S(1)}, f32[1,7,128,128]{3,2,1,0:T(8,128)}, u32[]{:S(2)}) copy-start(f32[1,7,128,128]{3,2,1,0:T(8,128)} %param.17) | copy-start | bytes 1376260
  85.8 12.0 %copy-start.1 = (f32[1,8,128,128]{3,2,1,0:T(8,128)S(1)}, f32[1,8,128,128]{3,2,1,0:T(8,128)}, u32[]{:S(2)}) copy-start(f32[1,8,128,128]{3,2,1,0:T(8,128)} %param.15) | copy-start | bytes 1572868
  100.9 0.6 copy-start.3
  224.1 0.6 copy-start.4
Sparse Core Ops, SparseCore 0:
  101.7 34.2 all-gather.3
where the time goes:
time: 233 us; the launch traced here: 232 us
  blocking collectives  123 us (53%)
  matrix products  38.5 us (17%)
  waiting for transfers between devices  33.8 us (15%)
  between operations  16.3 us (7%)
  local copies, waits for them, and re-layouts  14.4 us (6%)
  other arithmetic  5.94 us (3%)
    psum x2, blocking collectives, local(): total_drag = lax.psum(partial_drag, ('group', 'strip'))  80.9 us
    all_gather x2, blocking collectives, local(): lax.all_gather(force_rows, 'strip', axis=0, tiled=True)  41.6 us
    dot_general x58, matrix products, apply_block(): lax.dot_general(vectors, matrix, (((1,), (1,)), ((), ())), precision=EXAC...  38 us
    all_gather x1, waiting for transfers between devices, local(): lax.all_gather(displacement[None], 'strip', axis=0, tiled=True)  33.8 us
  transfers between devices with their start and end apart: 1, of which 1 were waited for; matrix products, arithmetic and copies ran while one was open for 0% of the time, Pallas kernels for 0%

commit v1 on v0

--- a/solution.py
+++ b/solution.py
@@ -109,7 +109,8 @@
     for coupled_step in range(COUPLED):
         vorticity, force_rows = strip_step(vorticity, flow_x, flow_y, motion, kernels, substeps)
         partial_drag = jnp.sum(force_rows[:, substeps:], axis=0)
-        total_drag = lax.psum(partial_drag, ("group", "strip"))
+        parts = lax.all_gather(partial_drag, ("group", "strip"))
+        total_drag = jnp.sum(parts, axis=0)
         offset = total_drag / jnp.sqrt(jnp.float32(total_strips))
         beam_load = first_contract(
             lax.all_gather(force_rows, "strip", axis=0, tiled=True), node_hit

time: 233 us -> 234 us (level)
    psum x2 -> x0, blocking collectives: 80.9 us -> none  [local(): total_drag = lax.psum(partial_drag, ('group', 'strip'))]
    unnamed x0 -> x2, blocking collectives: none -> 80.8 us
where the time goes in v1:
time: 234 us; the launch traced here: 232 us
  blocking collectives  122 us (52%)
  matrix products  38.5 us (16%)
  waiting for transfers between devices  33.8 us (14%)
  between operations  16.3 us (7%)
  local copies, waits for them, and re-layouts  15 us (6%)
  other arithmetic  6 us (3%)
    unnamed x2, blocking collectives  80.8 us
    all_gather x2, blocking collectives, local(): lax.all_gather(force_rows, 'strip', axis=0, tiled=True)  41.6 us
    dot_general x58, matrix products, apply_block(): lax.dot_general(vectors, matrix, (((1,), (1,)), ((), ())), precision=EXAC...  38 us
    all_gather x1, waiting for transfers between devices, local(): lax.all_gather(displacement[None], 'strip', axis=0, tiled=True)  33.8 us
  transfers between devices with their start and end apart: 1, of which 1 were waited for; matrix products, arithmetic and copies ran while one was open for 0% of the time, Pallas kernels for 0%

profile of v1, /device:TPU:0, one launch (start us, length us, event | category | flops | bytes accessed | tf_op | source)
XLA Modules:
  0.0 232.2 jit_solution(10416403958677210791)
XLA Ops:
  16.2 42.0 %all-reduce.1 = f32[256]{0:T(256)S(1)} all-reduce(f32[256]{0:T(256)S(1)} %dynamic-update-slice.8), channel_id=2, replica_groups=mesh['group'=2,'strip'=16] {'group','strip'}, use_global_device_ids=true, to_apply=%add.1 | all-reduce | flops 256 | bytes 2048
  59.1 21.0 %all-gather.2 = f32[16,2,16]{2,1,0:T(2,128)S(1)} all-gather(f32[1,2,16]{2,1,0:T(2,128)S(1)} %bitcast.564), channel_id=1, replica_groups=mesh['group'=2,'strip'=16] {'strip'}, dimensions={0}, use_global_device_ids=true | all-gather | bytes 2176 | tf_op jit(solution)/shard_map/all_gather | solution.py:116
  82.9 1.1 convolution_subtract_fusion.27
  83.9 1.1 fusion.159
  85.0 1.1 convolution_subtract_fusion.26
  86.2 1.1 fusion.149
  87.3 1.1 convolution_subtract_fusion.25
  88.3 1.1 fusion.139
  89.4 1.1 convolution_subtract_fusion.24
  90.4 1.1 fusion.129
  91.5 1.1 convolution_subtract_fusion.23
  92.6 1.1 fusion.119
  93.6 1.1 convolution_subtract_fusion.22
  94.7 1.1 fusion.109
  95.7 1.1 convolution_subtract_fusion.21
  96.8 1.1 fusion.99
  102.5 33.8 %all-gather.6.cloned.1.call-done = f32[16,16,1024]{2,1,0:T(8,128)} async-done(((f32[1,16,1024]{2,1,0:T(8,128)}), f32[16,16,1024]{2,1,0:T(8,128)}) %all-gather.6.cloned.1.call-update) | async-done | bytes 1048592 | tf_op jit(solution)/shard_map/all_gather | solution.py:121
  136.3 1.8 gather_fusion
  142.5 1.1 multiply_reduce_fusion.7
  144.7 38.9 %all-reduce.2 = f32[256]{0:T(256)S(1)} all-reduce(f32[256]{0:T(256)S(1)} %dynamic-update-slice.9), channel_id=3, replica_groups=mesh['group'=2,'strip'=16] {'group','strip'}, use_global_device_ids=true, to_apply=%add.2 | all-reduce | flops 256 | bytes 2048
  184.6 20.6 %all-gather.3 = f32[16,2,16]{2,1,0:T(2,128)S(1)} all-gather(f32[1,2,16]{2,1,0:T(2,128)S(1)} %bitcast.565), channel_id=1, replica_groups=mesh['group'=2,'strip'=16] {'strip'}, dimensions={0}, use_global_device_ids=true | all-gather | bytes 2176 | tf_op jit(solution)/shard_map/all_gather | solution.py:116
  206.5 1.1 convolution_subtract_fusion.13
  207.6 1.1 fusion.155
  208.6 1.1 convolution_subtract_fusion.12
  210.8 1.1 convolution_subtract_fusion.11
  211.8 1.1 fusion.135
  212.9 1.1 convolution_subtract_fusion.10
  213.9 1.1 fusion.125
  215.0 1.1 convolution_subtract_fusion.9
  217.1 1.1 convolution_subtract_fusion.8
  219.3 1.1 convolution_subtract_fusion.7
  220.3 1.1 fusion.97
  (228 shorter events, 30.1 us)
Async XLA Ops:
  7.2 129.1 %all-gather.6.cloned.1.call-start = ((), (), s32[]{:S(2)}) async-start(), calls=%async_computation | async-start | bytes 1114112 | tf_op jit(solution)/shard_map/all_gather | solution.py:121
  8.3 1.0 copy-start
  80.1 0.7 copy-start.6
  80.1 0.7 copy-start.7
  80.9 0.7 copy-start.5
  85.0 12.9 %copy-start.2 = (f32[1,7,128,128]{3,2,1,0:T(8,128)S(1)}, f32[1,7,128,128]{3,2,1,0:T(8,128)}, u32[]{:S(2)}) copy-start(f32[1,7,128,128]{3,2,1,0:T(8,128)} %param.17) | copy-start | bytes 1376260
  86.1 12.0 %copy-start.1 = (f32[1,8,128,128]{3,2,1,0:T(8,128)S(1)}, f32[1,8,128,128]{3,2,1,0:T(8,128)}, u32[]{:S(2)}) copy-start(f32[1,8,128,128]{3,2,1,0:T(8,128)} %param.15) | copy-start | bytes 1572868
  101.2 0.6 copy-start.3
  224.7 0.6 copy-start.4
Sparse Core Ops, SparseCore 0:
  102.0 34.2 all-gather.5
